TPU v7x, 256 devices: a whole 4x4x8 slice. The times are simulated.
256 devices in a mesh: section: 4 (over x), seq: 16 (over z, y_hi), tp: 4 (over y_lo, core).
Axes of the slice: x: 4, y: 4 (y_hi: 2, y_lo: 2; y = y_hi * 2 + y_lo), z: 8, core: 2. Of those that a mesh axis runs over, the one named last changes fastest.
Arguments:
- queries: bfloat16 [4, 4096, 8192], P('section', 'seq', 'tp'), may hold values from -135 to 135
- upstream: bfloat16 [4, 4096, 8192], P('section', 'seq', 'tp'), may hold values from -48 to 48
- shared_kv: bfloat16 [2, 4096, 1024], P(None, ('seq', 'tp')), may hold values from -5 to 5
Outputs:
- d_queries: bfloat16 [4, 4096, 8192], P('section', 'seq', 'tp')
- d_shared_kv: float32 [2, 4096, 1024], P(None, ('seq', 'tp'))
All inputs are finite; a program needn't handle non-finite values.
Results may differ from a plain program's by a relative error of at most 0.0098.
Values may be sent and summed in bfloat16 or wider, within the bound.
No kernel may reach another device: no remote copies, remote signals or barrier semaphores. Data moves between devices by JAX's collectives and lax.ppermute only.
A program may use at most 128 MiB of HBM per device.

v0:
```python
import math
import jax
import jax.numpy as jnp
from jax import lax
from jax.sharding import PartitionSpec as P

QH = 64
KVH = 8
HD = 128
WINDOW = 1024


def shifted(value, axis, by):
    peers = lax.axis_size(axis)
    pairs = [(i, i + by) for i in range(peers) if 0 <= i + by < peers]
    return lax.ppermute(value, axis, pairs)


def head_grads(query_block, grad_block, keys_head, values_head, allowed, score_scale):
    scores = (
        jnp.einsum("rgd,ed->gre", query_block, keys_head, preferred_element_type=jnp.float32)
        * score_scale
    )
    masked = jnp.where(allowed[None], scores, -jnp.inf)
    highest = jnp.max(masked, axis=-1, keepdims=True)
    weights = jnp.exp(masked - highest)
    probs = weights / jnp.sum(weights, axis=-1, keepdims=True)
    probs_b = probs.astype(jnp.bfloat16)
    attn_out = jnp.einsum("gre,ed->rgd", probs_b, values_head, preferred_element_type=jnp.float32)
    delta = jnp.sum(grad_block.astype(jnp.float32) * attn_out, axis=-1)
    dprobs = jnp.einsum("rgd,ed->gre", grad_block, values_head, preferred_element_type=jnp.float32)
    dscores = probs * (dprobs - jnp.transpose(delta)[:, :, None])
    dscores_b = dscores.astype(jnp.bfloat16)
    grad_query = (
        jnp.einsum("gre,ed->rgd", dscores_b, keys_head, preferred_element_type=jnp.float32)
        * score_scale
    )
    grad_key = (
        jnp.einsum("gre,rgd->ed", dscores_b, query_block, preferred_element_type=jnp.float32)
        * score_scale
    )
    grad_value = jnp.einsum("gre,rgd->ed", probs_b, grad_block, preferred_element_type=jnp.float32)
    return (grad_query, grad_key, grad_value)


def body(queries, upstream, shared_kv):
    local_kv = lax.all_to_all(shared_kv, "tp", split_axis=2, concat_axis=1, tiled=True)
    tok_rows = local_kv.shape[1]
    kv_cols = local_kv.shape[2]
    head_size = HD
    local_kv_heads = kv_cols // head_size
    group_size = QH // KVH
    block_heads = max(1, group_size // 2)
    span_blocks = WINDOW // tok_rows
    score_scale = 1.0 / math.sqrt(head_size)
    earlier = [shifted(local_kv, "seq", span_blocks - offset) for offset in range(span_blocks)]
    extended = jnp.concatenate(earlier + [local_kv], axis=1)
    ext_rows = extended.shape[1]
    position = lax.axis_index("seq")
    row_ids = lax.broadcasted_iota(jnp.int32, (tok_rows, ext_rows), 0)
    key_ids = lax.broadcasted_iota(jnp.int32, (tok_rows, ext_rows), 1)
    allowed = (
        (key_ids >= row_ids + 1)
        & (key_ids <= row_ids + WINDOW)
        & (position * tok_rows - WINDOW + key_ids >= 0)
    )
    query_heads = queries.reshape(tok_rows, -1, head_size)
    grad_heads = upstream.reshape(tok_rows, -1, head_size)
    query_parts = []
    key_parts = []
    value_parts = []
    for kv_head in range(local_kv_heads):
        keys_head = extended[0, :, kv_head * head_size : (kv_head + 1) * head_size]
        values_head = extended[1, :, kv_head * head_size : (kv_head + 1) * head_size]
        key_total = jnp.zeros((ext_rows, head_size), jnp.float32)
        value_total = jnp.zeros((ext_rows, head_size), jnp.float32)
        for first_head in range(kv_head * group_size, (kv_head + 1) * group_size, block_heads):
            query_block = query_heads[:, first_head : first_head + block_heads]
            grad_block = grad_heads[:, first_head : first_head + block_heads]
            grad_query, grad_key, grad_value = head_grads(
                query_block, grad_block, keys_head, values_head, allowed, score_scale
            )
            query_parts.append(grad_query)
            key_total = key_total + grad_key
            value_total = value_total + grad_value
        key_parts.append(key_total)
        value_parts.append(value_total)
    d_queries = jnp.concatenate(query_parts, axis=1).reshape(1, tok_rows, -1).astype(jnp.bfloat16)
    grad_ext = jnp.stack([jnp.concatenate(key_parts, axis=1), jnp.concatenate(value_parts, axis=1)])
    own_rows = grad_ext[:, span_blocks * tok_rows :, :]
    for offset in range(span_blocks):
        own_rows = own_rows + shifted(
            grad_ext[:, offset * tok_rows : (offset + 1) * tok_rows, :].astype(jnp.bfloat16),
            "seq",
            offset - span_blocks,
        ).astype(jnp.float32)
    by_token = lax.all_to_all(own_rows, "tp", split_axis=1, concat_axis=2, tiled=True)
    sections = lax.axis_size("section")
    kinds, rows, cols = by_token.shape
    pieces = by_token.reshape(kinds, sections, rows // sections, cols)
    pieces = lax.all_to_all(pieces, "section", split_axis=1, concat_axis=1)
    chunk = pieces[:, 0]
    for other in range(1, sections):
        chunk = chunk + pieces[:, other]
    d_shared_kv = lax.all_gather(chunk, "section", axis=1, tiled=True)
    return (d_queries, d_shared_kv)


def solution(mesh):
    in_specs = (P("section", "seq", "tp"), P("section", "seq", "tp"), P(None, ("seq", "tp"), None))
    out_specs = (P("section", "seq", "tp"), P(None, ("seq", "tp"), None))
    return jax.shard_map(body, mesh=mesh, in_specs=in_specs, out_specs=out_specs, check_vma=False)
```

profile of v0, /device:TPU:80, one launch (start us, length us, event | category | flops | bytes accessed | tf_op | source)
XLA Modules:
  0.0 194.0 jit_solution(16692141543035240085)
XLA Ops:
  3.1 3.4 %all-to-all-start = ((bf16[4,2,16384]{2,1,0:T(2,128)(2,1)}), bf16[4,2,16384]{2,1,0:T(2,128)(2,1)S(1)}, u32[]{:S(2)}, u32[]{:S(2)}) async-start(bf16[4,2,16384]{2,1,0:T(2,128)(2,1)} %reshape.114), calls=%async_computation | async-start | bytes 524288 | tf_op jit(solution)/shard_map/all_to_all | solution.py:47
  6.5 5.9 %all-to-all-done = bf16[4,2,16384]{2,1,0:T(2,128)(2,1)S(1)} async-done(((bf16[4,2,16384]{2,1,0:T(2,128)(2,1)}), bf16[4,2,16384]{2,1,0:T(2,128)(2,1)S(1)}, u32[]{:S(2)}, u32[]{:S(2)}) %all-to-all-start) | async-done | bytes 262176 | tf_op jit(solution)/shard_map/all_to_all | solution.py:47
  13.8 6.4 %collective-permute-start = (bf16[2,256,256]{2,1,0:T(8,128)(2,1)}, bf16[2,256,256]{2,1,0:T(8,128)(2,1)}, u32[]{:S(2)}, u32[]{:S(2)}) collective-permute-start(bf16[2,256,256]{2,1,0:T(8,128)(2,1)} %bitcast.2), channel_id=1, source_target_pairs={{0,16},{4,20},{8,24},{12,28},{16,32},{20,36},{24,40},{28,44},{32,4... | collective-permute-start | bytes 786440 | tf_op jit(solution)/shard_map/ppermute | solution.py:16
  21.9 2.9 %collective-permute-start.2 = (bf16[2,256,256]{2,1,0:T(8,128)(2,1)}, bf16[2,256,256]{2,1,0:T(8,128)(2,1)}, u32[]{:S(2)}, u32[]{:S(2)}) collective-permute-start(bf16[2,256,256]{2,1,0:T(8,128)(2,1)} %bitcast.2), channel_id=1, source_target_pairs={{0,8},{4,12},{8,16},{12,20},{16,24},{20,28},{24,32},{28,36},{32,40... | collective-permute-start | bytes 786440 | tf_op jit(solution)/shard_map/ppermute | solution.py:16
  24.8 3.2 %collective-permute-start.1 = (bf16[2,256,256]{2,1,0:T(8,128)(2,1)}, bf16[2,256,256]{2,1,0:T(8,128)(2,1)}, u32[]{:S(2)}, u32[]{:S(2)}) collective-permute-start(bf16[2,256,256]{2,1,0:T(8,128)(2,1)} %bitcast.2), channel_id=1, source_target_pairs={{0,12},{4,16},{8,20},{12,24},{16,28},{20,32},{24,36},{28,40},{32,4... | collective-permute-start | bytes 786440 | tf_op jit(solution)/shard_map/ppermute | solution.py:16
  28.1 1.5 copy.95
  33.1 5.3 %collective-permute-start.3 = (bf16[2,256,256]{2,1,0:T(8,128)(2,1)}, bf16[2,256,256]{2,1,0:T(8,128)(2,1)S(1)}, u32[]{:S(2)}, u32[]{:S(2)}) collective-permute-start(bf16[2,256,256]{2,1,0:T(8,128)(2,1)} %bitcast.2), channel_id=1, source_target_pairs={{0,4},{4,8},{8,12},{12,16},{16,20},{20,24},{24,28},{28,32},{32,36}... | collective-permute-start | bytes 786440 | tf_op jit(solution)/shard_map/ppermute | solution.py:16
  39.4 10.3 %collective-permute-done.1 = bf16[2,256,256]{2,1,0:T(8,128)(2,1)} collective-permute-done((bf16[2,256,256]{2,1,0:T(8,128)(2,1)}, bf16[2,256,256]{2,1,0:T(8,128)(2,1)}, u32[]{:S(2)}, u32[]{:S(2)}) %collective-permute-start.1) | collective-permute-done | bytes 262176 | tf_op jit(solution)/shard_map/ppermute | solution.py:16
  51.6 2.3 %collective-permute-done.3 = bf16[2,256,256]{2,1,0:T(8,128)(2,1)S(1)} collective-permute-done((bf16[2,256,256]{2,1,0:T(8,128)(2,1)}, bf16[2,256,256]{2,1,0:T(8,128)(2,1)S(1)}, u32[]{:S(2)}, u32[]{:S(2)}) %collective-permute-start.3) | collective-permute-done | bytes 262176 | tf_op jit(solution)/shard_map/ppermute | solution.py:16
  54.9 5.3 %exponential_reduce_fusion.3 = (f32[4,256]{1,0:T(4,128)S(1)}, f32[4,256,1280]{1,2,0:T(8,128)}) fusion(pred[256,1280]{0,1:T(8,128)(4,1)} %fusion.28, bf16[256,16,128]{0,2,1:T(8,128)(2,1)S(1)} %bitcast.226, bf16[2,1280,256]{2,1,0:T(8,128)(2,1)S(1)} %constant_dynamic-update-slice_fusion), kind=kOutput, calls=%fused_computation.31 | convolution fusion | flops 340788480 | bytes 6164480 | tf_op jit(solution)/shard_map/sub | solution.py:26
  60.2 5.1 %exponential_reduce_fusion.1 = (f32[4,256]{1,0:T(4,128)S(1)}, f32[4,256,1280]{1,2,0:T(8,128)}) fusion(pred[256,1280]{0,1:T(8,128)(4,1)} %fusion.28, bf16[256,16,128]{0,2,1:T(8,128)(2,1)S(1)} %bitcast.227, bf16[2,1280,256]{2,1,0:T(8,128)(2,1)S(1)} %constant_dynamic-update-slice_fusion), kind=kOutput, calls=%fused_computation.27 | convolution fusion | flops 340788480 | bytes 6164480 | tf_op jit(solution)/shard_map/sub | solution.py:26
  65.3 5.1 %exponential_reduce_fusion.2 = (f32[4,256]{1,0:T(4,128)S(1)}, f32[4,256,1280]{1,2,0:T(8,128)}) fusion(pred[256,1280]{0,1:T(8,128)(4,1)} %fusion.28, bf16[256,16,128]{0,2,1:T(8,128)(2,1)S(1)} %bitcast.228, bf16[2,1280,256]{2,1,0:T(8,128)(2,1)S(1)} %constant_dynamic-update-slice_fusion), kind=kOutput, calls=%fused_computation.29 | convolution fusion | flops 340788480 | bytes 6164480 | tf_op jit(solution)/shard_map/sub | solution.py:26
  70.4 5.1 %exponential_reduce_fusion = (f32[4,256]{1,0:T(4,128)S(1)}, f32[4,256,1280]{1,2,0:T(8,128)}) fusion(pred[256,1280]{0,1:T(8,128)(4,1)} %fusion.28, bf16[256,16,128]{0,2,1:T(8,128)(2,1)S(1)} %bitcast.229, bf16[2,1280,256]{2,1,0:T(8,128)(2,1)S(1)} %constant_dynamic-update-slice_fusion), kind=kOutput, calls=%fused_computation.25 | convolution fusion | flops 340788480 | bytes 6164480 | tf_op jit(solution)/shard_map/sub | solution.py:26
  75.5 4.0 %fusion.23 = bf16[4,256,1280]{1,2,0:T(8,128)(2,1)S(1)} fusion(f32[4,256]{1,0:T(4,128)S(1)} %get-tuple-element.22, f32[4,256,1280]{1,2,0:T(8,128)} %get-tuple-element.23), kind=kLoop, calls=%fused_computation.50 | loop fusion | flops 2621440 | bytes 7868416 | tf_op jit(solution)/shard_map/convert_element_type | solution.py:28
  84.2 1.6 fusion.25
  102.8 2.5 %fusion.9 = bf16[4,256,1280]{1,2,0:T(8,128)(2,1)S(1)} fusion(f32[4,256]{1,0:T(4,128)S(1)} %bitcast.239, f32[4,256]{1,0:T(4,128)S(1)} %get-tuple-element.16, f32[4,256,1280]{1,2,0:T(8,128)S(1)} %bitcast.219, bf16[2,1280,256]{2,1,0:T(8,128)(2,1)S(1)} %copy-done.5, bf16[256,16,128]{0,2,1:T(8,128)(2,1)} %bitcast.217), kind=kOutput, calls=%fused_computation.10 | convolution fusion | flops 340787200 | bytes 8462336 | tf_op jit(solution)/shard_map/rgd,ed->gre/dot_general | solution.py:31
  107.7 1.9 collective-permute-start.4
  109.6 3.8 %collective-permute-start.7 = (bf16[2,256,256]{1,2,0:T(8,128)(2,1)S(1)}, bf16[2,256,256]{1,2,0:T(8,128)(2,1)S(1)}, u32[]{:S(2)}, u32[]{:S(2)}) collective-permute-start(bf16[2,256,256]{1,2,0:T(8,128)(2,1)S(1)} %get-tuple-element.9), channel_id=1, source_target_pairs={{4,0},{8,4},{12,8},{16,12},{20,16},{24,20},{28,24},{32,28},{36,32}... | collective-permute-start | bytes 786440 | tf_op jit(solution)/shard_map/ppermute | solution.py:16
  113.4 1.9 collective-permute-start.6
  115.3 1.9 collective-permute-start.5
  117.8 8.0 %collective-permute-done.4 = bf16[2,256,256]{1,2,0:T(8,128)(2,1)S(1)} collective-permute-done((bf16[2,256,256]{1,2,0:T(8,128)(2,1)S(1)}, bf16[2,256,256]{1,2,0:T(8,128)(2,1)S(1)}, u32[]{:S(2)}, u32[]{:S(2)}) %collective-permute-start.4) | collective-permute-done | bytes 262176 | tf_op jit(solution)/shard_map/ppermute | solution.py:16
  125.8 7.0 %collective-permute-done.7 = bf16[2,256,256]{1,2,0:T(8,128)(2,1)S(1)} collective-permute-done((bf16[2,256,256]{1,2,0:T(8,128)(2,1)S(1)}, bf16[2,256,256]{1,2,0:T(8,128)(2,1)S(1)}, u32[]{:S(2)}, u32[]{:S(2)}) %collective-permute-start.7) | collective-permute-done | bytes 262176 | tf_op jit(solution)/shard_map/ppermute | solution.py:16
  132.8 17.3 %collective-permute-done.5 = bf16[2,256,256]{1,2,0:T(8,128)(2,1)S(1)} collective-permute-done((bf16[2,256,256]{1,2,0:T(8,128)(2,1)S(1)}, bf16[2,256,256]{1,2,0:T(8,128)(2,1)S(1)}, u32[]{:S(2)}, u32[]{:S(2)}) %collective-permute-start.5) | collective-permute-done | bytes 262176 | tf_op jit(solution)/shard_map/ppermute | solution.py:16
  151.3 3.5 %all-to-all-start.1 = ((f32[2,256,256]{2,0,1:T(2,128)}), f32[2,256,256]{2,0,1:T(2,128)S(1)}, u32[]{:S(2)}, u32[]{:S(2)}) async-start(f32[2,256,256]{2,0,1:T(2,128)} %copy.141), calls=%async_computation.1 | async-start | bytes 1048576 | tf_op jit(solution)/shard_map/all_to_all | solution.py:97
  154.8 3.2 %fusion.42 = bf16[256,4,128]{0,2,1:T(8,128)(2,1)} fusion(bf16[4,256,1280]{1,2,0:T(8,128)(2,1)} %copy-done.2, bf16[2,1280,256]{2,1,0:T(8,128)(2,1)} %copy-done.4), kind=kOutput, calls=%fused_computation.81 | convolution fusion | flops 335806464 | bytes 3211264 | tf_op jit(solution)/shard_map/gre,ed->rgd/dot_general | solution.py:35
  158.0 2.2 %fusion.43 = bf16[256,4,128]{0,2,1:T(8,128)(2,1)} fusion(bf16[4,256,1280]{1,2,0:T(8,128)(2,1)S(1)} %copy-done.1, bf16[2,1280,256]{2,1,0:T(8,128)(2,1)} %copy-done.4), kind=kOutput, calls=%fused_computation.82 | convolution fusion | flops 335806464 | bytes 3211264 | tf_op jit(solution)/shard_map/gre,ed->rgd/dot_general | solution.py:35
  160.2 3.3 %all-to-all-done.1 = f32[2,256,256]{2,0,1:T(2,128)S(1)} async-done(((f32[2,256,256]{2,0,1:T(2,128)}), f32[2,256,256]{2,0,1:T(2,128)S(1)}, u32[]{:S(2)}, u32[]{:S(2)}) %all-to-all-start.1) | async-done | bytes 524320 | tf_op jit(solution)/shard_map/all_to_all | solution.py:97
  165.0 1.9 copy.144
  166.9 4.3 %all-to-all-start.2 = ((f32[2,4,16,1024]{3,2,0,1:T(8,128)}), f32[2,4,16,1024]{3,2,0,1:T(8,128)S(1)}, u32[]{:S(2)}, u32[]{:S(2)}) async-start(f32[2,4,16,1024]{3,2,0,1:T(8,128)} %copy.144), calls=%async_computation.2 | async-start | bytes 1048576 | tf_op jit(solution)/shard_map/all_to_all | solution.py:101
  171.2 1.6 fusion.41
  174.3 6.0 %all-to-all-done.2 = f32[2,4,16,1024]{3,2,0,1:T(8,128)S(1)} async-done(((f32[2,4,16,1024]{3,2,0,1:T(8,128)}), f32[2,4,16,1024]{3,2,0,1:T(8,128)S(1)}, u32[]{:S(2)}, u32[]{:S(2)}) %all-to-all-start.2) | async-done | bytes 524320 | tf_op jit(solution)/shard_map/all_to_all | solution.py:101
  180.4 12.8 %all-gather = f32[2,1,64,1024]{3,2,0,1:T(8,128)S(1)} all-gather(f32[2,1,16,1024]{3,2,0,1:T(8,128)S(1)} %slice_add_fusion), channel_id=2, replica_groups=mesh['section'=4,'seq'=16,'tp'=4] {'section'}, dimensions={2}, use_global_device_ids=true | all-gather | bytes 655360 | tf_op jit(solution)/shard_map/all_gather | solution.py:105
  (102 shorter events, 42.3 us)
Async XLA Ops:
  0.6 20.7 %copy-start.12 = (bf16[1,256,2048]{2,1,0:T(8,128)(2,1)S(1)}, bf16[1,256,2048]{2,1,0:T(8,128)(2,1)}, u32[]{:S(2)}) copy-start(bf16[1,256,2048]{2,1,0:T(8,128)(2,1)} %param.4) | copy-start | bytes 3145732
  3.1 9.4 %all-to-all-start = ((bf16[4,2,16384]{2,1,0:T(2,128)(2,1)}), bf16[4,2,16384]{2,1,0:T(2,128)(2,1)S(1)}, u32[]{:S(2)}, u32[]{:S(2)}) async-start(bf16[4,2,16384]{2,1,0:T(2,128)(2,1)} %reshape.114), calls=%async_computation | async-start | bytes 524288 | tf_op jit(solution)/shard_map/all_to_all | solution.py:47
  13.8 24.6 %collective-permute-start = (bf16[2,256,256]{2,1,0:T(8,128)(2,1)}, bf16[2,256,256]{2,1,0:T(8,128)(2,1)}, u32[]{:S(2)}, u32[]{:S(2)}) collective-permute-start(bf16[2,256,256]{2,1,0:T(8,128)(2,1)} %bitcast.2), channel_id=1, source_target_pairs={{0,16},{4,20},{8,24},{12,28},{16,32},{20,36},{24,40},{28,44},{32,4... | collective-permute-start | bytes 786440 | tf_op jit(solution)/shard_map/ppermute | solution.py:16
  21.9 79.6 %copy-start.3 = (bf16[1,256,2048]{1,2,0:T(8,128)(2,1)}, bf16[1,256,2048]{1,2,0:T(8,128)(2,1)S(1)}, u32[]{:S(2)}) copy-start(bf16[1,256,2048]{1,2,0:T(8,128)(2,1)S(1)} %copy.97) | copy-start | bytes 3145732
  21.9 28.7 %collective-permute-start.2 = (bf16[2,256,256]{2,1,0:T(8,128)(2,1)}, bf16[2,256,256]{2,1,0:T(8,128)(2,1)}, u32[]{:S(2)}, u32[]{:S(2)}) collective-permute-start(bf16[2,256,256]{2,1,0:T(8,128)(2,1)} %bitcast.2), channel_id=1, source_target_pairs={{0,8},{4,12},{8,16},{12,20},{16,24},{20,28},{24,32},{28,36},{32,40... | collective-permute-start | bytes 786440 | tf_op jit(solution)/shard_map/ppermute | solution.py:16
  24.8 24.8 %collective-permute-start.1 = (bf16[2,256,256]{2,1,0:T(8,128)(2,1)}, bf16[2,256,256]{2,1,0:T(8,128)(2,1)}, u32[]{:S(2)}, u32[]{:S(2)}) collective-permute-start(bf16[2,256,256]{2,1,0:T(8,128)(2,1)} %bitcast.2), channel_id=1, source_target_pairs={{0,12},{4,16},{8,20},{12,24},{16,28},{20,32},{24,36},{28,40},{32,4... | collective-permute-start | bytes 786440 | tf_op jit(solution)/shard_map/ppermute | solution.py:16
  29.6 59.7 %copy-start.6 = (bf16[1,256,2048]{1,2,0:T(8,128)(2,1)}, bf16[1,256,2048]{1,2,0:T(8,128)(2,1)S(1)}, u32[]{:S(2)}) copy-start(bf16[1,256,2048]{1,2,0:T(8,128)(2,1)S(1)} %copy.95) | copy-start | bytes 3145732
  33.1 20.8 %collective-permute-start.3 = (bf16[2,256,256]{2,1,0:T(8,128)(2,1)}, bf16[2,256,256]{2,1,0:T(8,128)(2,1)S(1)}, u32[]{:S(2)}, u32[]{:S(2)}) collective-permute-start(bf16[2,256,256]{2,1,0:T(8,128)(2,1)} %bitcast.2), channel_id=1, source_target_pairs={{0,4},{4,8},{8,12},{12,16},{16,20},{20,24},{24,28},{28,32},{32,36}... | collective-permute-start | bytes 786440 | tf_op jit(solution)/shard_map/ppermute | solution.py:16
  54.9 45.3 %copy-start.4 = (bf16[2,1280,256]{2,1,0:T(8,128)(2,1)}, bf16[2,1280,256]{2,1,0:T(8,128)(2,1)S(1)}, u32[]{:S(2)}) copy-start(bf16[2,1280,256]{2,1,0:T(8,128)(2,1)S(1)} %constant_dynamic-update-slice_fusion) | copy-start | bytes 3932164
  75.5 6.3 %slice-start.6 = ((s8[5242880]{0:T(1024)(128)(4,1)}), s8[4194304]{0:T(1024)(128)(4,1)S(1)}, s32[]{:S(2)}) async-start(s8[5242880]{0:T(1024)(128)(4,1)} %bitcast.224), calls=%async_computation.9 | async-start | bytes 8388608
  79.5 2.3 %slice-start.7 = ((s8[5242880]{0:T(1024)(128)(4,1)}), s8[1048576]{0:T(1024)(128)(4,1)S(1)}, s32[]{:S(2)}) async-start(s8[5242880]{0:T(1024)(128)(4,1)} %bitcast.224), calls=%async_computation.10 | async-start | bytes 2097152
  81.7 2.2 %slice-start.4 = ((s8[5242880]{0:T(1024)(128)(4,1)}), s8[4194304]{0:T(1024)(128)(4,1)S(1)}, s32[]{:S(2)}) async-start(s8[5242880]{0:T(1024)(128)(4,1)} %bitcast.222), calls=%async_computation.7 | async-start | bytes 8388608
  81.8 2.5 %slice-start.5 = ((s8[5242880]{0:T(1024)(128)(4,1)}), s8[1048576]{0:T(1024)(128)(4,1)S(1)}, s32[]{:S(2)}) async-start(s8[5242880]{0:T(1024)(128)(4,1)} %bitcast.222), calls=%async_computation.8 | async-start | bytes 2097152
  88.1 2.7 %slice-start.2 = ((s8[5242880]{0:T(1024)(128)(4,1)}), s8[4194304]{0:T(1024)(128)(4,1)S(1)}, s32[]{:S(2)}) async-start(s8[5242880]{0:T(1024)(128)(4,1)} %bitcast.220), calls=%async_computation.5 | async-start | bytes 8388608
  88.1 3.4 %slice-start.3 = ((s8[5242880]{0:T(1024)(128)(4,1)}), s8[1048576]{0:T(1024)(128)(4,1)S(1)}, s32[]{:S(2)}) async-start(s8[5242880]{0:T(1024)(128)(4,1)} %bitcast.220), calls=%async_computation.6 | async-start | bytes 2097152
  89.3 1.6 copy-start.2
  91.6 1.4 copy-start.9
  95.3 2.4 %slice-start = ((s8[5242880]{0:T(1024)(128)(4,1)}), s8[4194304]{0:T(1024)(128)(4,1)S(1)}, s32[]{:S(2)}) async-start(s8[5242880]{0:T(1024)(128)(4,1)} %bitcast.218), calls=%async_computation.3 | async-start | bytes 8388608
  95.3 3.4 %slice-start.1 = ((s8[5242880]{0:T(1024)(128)(4,1)}), s8[1048576]{0:T(1024)(128)(4,1)S(1)}, s32[]{:S(2)}) async-start(s8[5242880]{0:T(1024)(128)(4,1)} %bitcast.218), calls=%async_computation.4 | async-start | bytes 2097152
  96.4 8.8 %copy-start = (bf16[4,256,1280]{1,2,0:T(8,128)(2,1)}, bf16[4,256,1280]{1,2,0:T(8,128)(2,1)S(1)}, u32[]{:S(2)}) copy-start(bf16[4,256,1280]{1,2,0:T(8,128)(2,1)S(1)} %fusion.13) | copy-start | bytes 7864324
  98.7 1.4 copy-start.8
  101.4 1.3 copy-start.5
  102.8 2.5 %copy-start.7 = (bf16[1,256,2048]{1,2,0:T(8,128)(2,1)S(1)}, bf16[1,256,2048]{1,2,0:T(8,128)(2,1)}, u32[]{:S(2)}) copy-start(bf16[1,256,2048]{1,2,0:T(8,128)(2,1)} %copy-done.6) | copy-start | bytes 3145732
  107.7 18.1 %collective-permute-start.4 = (bf16[2,256,256]{1,2,0:T(8,128)(2,1)S(1)}, bf16[2,256,256]{1,2,0:T(8,128)(2,1)S(1)}, u32[]{:S(2)}, u32[]{:S(2)}) collective-permute-start(bf16[2,256,256]{1,2,0:T(8,128)(2,1)S(1)} %get-tuple-element.8), channel_id=1, source_target_pairs={{16,0},{20,4},{24,8},{28,12},{32,16},{36,20},{40,24},{44,28},{48,3... | collective-permute-start | bytes 786440 | tf_op jit(solution)/shard_map/ppermute | solution.py:16
  109.6 23.2 %collective-permute-start.7 = (bf16[2,256,256]{1,2,0:T(8,128)(2,1)S(1)}, bf16[2,256,256]{1,2,0:T(8,128)(2,1)S(1)}, u32[]{:S(2)}, u32[]{:S(2)}) collective-permute-start(bf16[2,256,256]{1,2,0:T(8,128)(2,1)S(1)} %get-tuple-element.9), channel_id=1, source_target_pairs={{4,0},{8,4},{12,8},{16,12},{20,16},{24,20},{28,24},{32,28},{36,32}... | collective-permute-start | bytes 786440 | tf_op jit(solution)/shard_map/ppermute | solution.py:16
  113.4 19.4 %collective-permute-start.6 = (bf16[2,256,256]{1,2,0:T(8,128)(2,1)S(1)}, bf16[2,256,256]{1,2,0:T(8,128)(2,1)S(1)}, u32[]{:S(2)}, u32[]{:S(2)}) collective-permute-start(bf16[2,256,256]{1,2,0:T(8,128)(2,1)S(1)} %get-tuple-element.10), channel_id=1, source_target_pairs={{8,0},{12,4},{16,8},{20,12},{24,16},{28,20},{32,24},{36,28},{40,32... | collective-permute-start | bytes 786440 | tf_op jit(solution)/shard_map/ppermute | solution.py:16
  115.3 34.8 %collective-permute-start.5 = (bf16[2,256,256]{1,2,0:T(8,128)(2,1)S(1)}, bf16[2,256,256]{1,2,0:T(8,128)(2,1)S(1)}, u32[]{:S(2)}, u32[]{:S(2)}) collective-permute-start(bf16[2,256,256]{1,2,0:T(8,128)(2,1)S(1)} %get-tuple-element.11), channel_id=1, source_target_pairs={{12,0},{16,4},{20,8},{24,12},{28,16},{32,20},{36,24},{40,28},{44,3... | collective-permute-start | bytes 786440 | tf_op jit(solution)/shard_map/ppermute | solution.py:16
  151.3 12.3 %all-to-all-start.1 = ((f32[2,256,256]{2,0,1:T(2,128)}), f32[2,256,256]{2,0,1:T(2,128)S(1)}, u32[]{:S(2)}, u32[]{:S(2)}) async-start(f32[2,256,256]{2,0,1:T(2,128)} %copy.141), calls=%async_computation.1 | async-start | bytes 1048576 | tf_op jit(solution)/shard_map/all_to_all | solution.py:97
  154.8 3.2 %copy-start.1 = (bf16[4,256,1280]{1,2,0:T(8,128)(2,1)S(1)}, bf16[4,256,1280]{1,2,0:T(8,128)(2,1)}, u32[]{:S(2)}) copy-start(bf16[4,256,1280]{1,2,0:T(8,128)(2,1)} %copy-done) | copy-start | bytes 7864324
  166.9 13.5 %all-to-all-start.2 = ((f32[2,4,16,1024]{3,2,0,1:T(8,128)}), f32[2,4,16,1024]{3,2,0,1:T(8,128)S(1)}, u32[]{:S(2)}, u32[]{:S(2)}) async-start(f32[2,4,16,1024]{3,2,0,1:T(8,128)} %copy.144), calls=%async_computation.2 | async-start | bytes 1048576 | tf_op jit(solution)/shard_map/all_to_all | solution.py:101
  171.2 1.6 copy-start.13
  171.2 1.6 copy-start.14
  (2 other events, 2.0 us)
where the time goes:
time: 195 us; the launch traced here: 194 us
  waiting for transfers between devices  60.1 us (31%)
  matrix products  46.9 us (24%)
  starting transfers between devices  38.4 us (20%)
  local copies, waits for them, and re-layouts  24.2 us (12%)
  blocking collectives  12.8 us (7%)
  other arithmetic  10.2 us (5%)
    ppermute x8, waiting for transfers between devices, shifted(): return lax.ppermute(value, axis, pairs)  44.8 us
    ppermute x8, starting transfers between devices, shifted(): return lax.ppermute(value, axis, pairs)  27.3 us
    sub x4, matrix products, head_grads(): weights = jnp.exp(masked - highest)  20.6 us
    unnamed x62, local copies, waits for them, and re-layouts  17.8 us
    all_gather x1, blocking collectives, body(): d_shared_kv = lax.all_gather(chunk, 'section', axis=1, tiled=True)  12.8 us
    convert_element_type x4, other arithmetic, head_grads(): probs_b = probs.astype(jnp.bfloat16)  8.43 us
    dot_general x4, matrix products, head_grads(): jnp.einsum('gre,ed->rgd', dscores_b, keys_head, preferred_element_type=jn...  7.58 us
    all_to_all x1, waiting for transfers between devices, body(): pieces = lax.all_to_all(pieces, 'section', split_axis=1, concat_axis=1)  6.01 us
  transfers between devices with their start and end apart: 11, of which 8 were waited for; matrix products, arithmetic and copies ran while one was open for 10% of the time, Pallas kernels for 0%

commit v1 on v0

--- a/solution.py
+++ b/solution.py
@@ -102,7 +102,16 @@
     chunk = pieces[:, 0]
     for other in range(1, sections):
         chunk = chunk + pieces[:, other]
-    d_shared_kv = lax.all_gather(chunk, "section", axis=1, tiled=True)
+    ways = lax.axis_size("section")
+    up = [(d, (d + 1) % ways) for d in range(ways)]
+    down = [(d, (d - 1) % ways) for d in range(ways)]
+    earlier_2, later = ([chunk], [chunk])
+    for _ in range(ways // 2):
+        earlier_2.append(lax.ppermute(earlier_2[-1], "section", up))
+    for _ in range((ways - 1) // 2):
+        later.append(lax.ppermute(later[-1], "section", down))
+    line = jnp.concatenate([*earlier_2[::-1], *later[1:]], axis=1)
+    d_shared_kv = jnp.roll(line, (lax.axis_index("section") - ways // 2) * chunk.shape[1], axis=1)
     return (d_queries, d_shared_kv)
 
 

time: 195 us -> 198 us (1.015)
  blocking collectives: 12.8 us -> 0 us
  waiting for transfers between devices: 60.1 us -> 68 us
  starting transfers between devices: 38.4 us -> 42.3 us
    all_gather x1 -> x0, blocking collectives: 12.8 us -> none  [body(): d_shared_kv = lax.all_gather(chunk, 'section', axis=1, tiled=True)]
    ppermute x0 -> x3, waiting for transfers between devices: none -> 6.54 us  [the longest x2 5.46 us: body(): earlier_2.append(lax.ppermute(earlier_2[-1], 'section', up))]
    ppermute x0 -> x3, starting transfers between devices: none -> 3.86 us  [the longest x1 3.21 us: body(): later.append(lax.ppermute(later[-1], 'section', down))]
    all_to_all x1, waiting for transfers between devices: 3.31 us -> 6.35 us  [body(): lax.all_to_all(own_rows, 'tp', split_axis=1, concat_axis=2, tiled=True)]
    all_to_all x1, waiting for transfers between devices: 6.01 us -> 3.73 us  [body(): pieces = lax.all_to_all(pieces, 'section', split_axis=1, concat_axis=1)]
    unnamed x62 -> x70, local copies, waits for them, and re-layouts: 17.8 us -> 17.7 us
  transfers between devices with their start and end apart: 11 -> 14, of which waited for: 8 -> 11; matrix products, arithmetic and copies ran while one was open for 10% -> 11% of each run, Pallas kernels for 0% -> 0%
where the time goes in v1:
time: 198 us; the launch traced here: 196 us
  waiting for transfers between devices  68 us (34%)
  matrix products  48.8 us (25%)
  starting transfers between devices  42.3 us (21%)
  local copies, waits for them, and re-layouts  24.9 us (13%)
  other arithmetic  10.3 us (5%)
    ppermute x8, waiting for transfers between devices, shifted(): return lax.ppermute(value, axis, pairs)  45.4 us
    ppermute x8, starting transfers between devices, shifted(): return lax.ppermute(value, axis, pairs)  27.3 us
    sub x4, matrix products, head_grads(): weights = jnp.exp(masked - highest)  20.6 us
    unnamed x70, local copies, waits for them, and re-layouts  17.7 us
    dot_general x4, matrix products, head_grads(): jnp.einsum('gre,ed->rgd', dscores_b, keys_head, preferred_element_type=jn...  9.35 us
    convert_element_type x4, other arithmetic, head_grads(): probs_b = probs.astype(jnp.bfloat16)  8.43 us
    all_to_all x1, waiting for transfers between devices, body(): lax.all_to_all(own_rows, 'tp', split_axis=1, concat_axis=2, tiled=True)  6.35 us
    all_to_all x1, waiting for transfers between devices, body(): lax.all_to_all(shared_kv, 'tp', split_axis=2, concat_axis=1, tiled=True)  5.94 us
  transfers between devices with their start and end apart: 14, of which 11 were waited for; matrix products, arithmetic and copies ran while one was open for 11% of the time, Pallas kernels for 0%

profile of v1, /device:TPU:80, one launch (start us, length us, event | category | flops | bytes accessed | tf_op | source)
XLA Modules:
  0.0 195.7 jit_solution(781189364204119263)
XLA Ops:
  3.1 3.4 %all-to-all-start = ((bf16[4,2,16384]{2,1,0:T(2,128)(2,1)}), bf16[4,2,16384]{2,1,0:T(2,128)(2,1)S(1)}, u32[]{:S(2)}, u32[]{:S(2)}) async-start(bf16[4,2,16384]{2,1,0:T(2,128)(2,1)} %reshape.113), calls=%async_computation | async-start | bytes 524288 | tf_op jit(solution)/shard_map/all_to_all | solution.py:47
  6.5 5.9 %all-to-all-done = bf16[4,2,16384]{2,1,0:T(2,128)(2,1)S(1)} async-done(((bf16[4,2,16384]{2,1,0:T(2,128)(2,1)}), bf16[4,2,16384]{2,1,0:T(2,128)(2,1)S(1)}, u32[]{:S(2)}, u32[]{:S(2)}) %all-to-all-start) | async-done | bytes 262176 | tf_op jit(solution)/shard_map/all_to_all | solution.py:47
  13.9 6.4 %collective-permute-start = (bf16[2,256,256]{2,1,0:T(8,128)(2,1)}, bf16[2,256,256]{2,1,0:T(8,128)(2,1)}, u32[]{:S(2)}, u32[]{:S(2)}) collective-permute-start(bf16[2,256,256]{2,1,0:T(8,128)(2,1)} %bitcast.2), channel_id=1, source_target_pairs={{0,16},{4,20},{8,24},{12,28},{16,32},{20,36},{24,40},{28,44},{32,4... | collective-permute-start | bytes 786440 | tf_op jit(solution)/shard_map/ppermute | solution.py:16
  21.9 2.9 %collective-permute-start.2 = (bf16[2,256,256]{2,1,0:T(8,128)(2,1)}, bf16[2,256,256]{2,1,0:T(8,128)(2,1)}, u32[]{:S(2)}, u32[]{:S(2)}) collective-permute-start(bf16[2,256,256]{2,1,0:T(8,128)(2,1)} %bitcast.2), channel_id=1, source_target_pairs={{0,8},{4,12},{8,16},{12,20},{16,24},{20,28},{24,32},{28,36},{32,40... | collective-permute-start | bytes 786440 | tf_op jit(solution)/shard_map/ppermute | solution.py:16
  24.8 3.2 %collective-permute-start.1 = (bf16[2,256,256]{2,1,0:T(8,128)(2,1)}, bf16[2,256,256]{2,1,0:T(8,128)(2,1)}, u32[]{:S(2)}, u32[]{:S(2)}) collective-permute-start(bf16[2,256,256]{2,1,0:T(8,128)(2,1)} %bitcast.2), channel_id=1, source_target_pairs={{0,12},{4,16},{8,20},{12,24},{16,28},{20,32},{24,36},{28,40},{32,4... | collective-permute-start | bytes 786440 | tf_op jit(solution)/shard_map/ppermute | solution.py:16
  33.1 5.3 %collective-permute-start.3 = (bf16[2,256,256]{2,1,0:T(8,128)(2,1)}, bf16[2,256,256]{2,1,0:T(8,128)(2,1)S(1)}, u32[]{:S(2)}, u32[]{:S(2)}) collective-permute-start(bf16[2,256,256]{2,1,0:T(8,128)(2,1)} %bitcast.2), channel_id=1, source_target_pairs={{0,4},{4,8},{8,12},{12,16},{16,20},{20,24},{24,28},{28,32},{32,36}... | collective-permute-start | bytes 786440 | tf_op jit(solution)/shard_map/ppermute | solution.py:16
  39.4 10.3 %collective-permute-done.1 = bf16[2,256,256]{2,1,0:T(8,128)(2,1)} collective-permute-done((bf16[2,256,256]{2,1,0:T(8,128)(2,1)}, bf16[2,256,256]{2,1,0:T(8,128)(2,1)}, u32[]{:S(2)}, u32[]{:S(2)}) %collective-permute-start.1) | collective-permute-done | bytes 262176 | tf_op jit(solution)/shard_map/ppermute | solution.py:16
  51.6 2.3 %collective-permute-done.3 = bf16[2,256,256]{2,1,0:T(8,128)(2,1)S(1)} collective-permute-done((bf16[2,256,256]{2,1,0:T(8,128)(2,1)}, bf16[2,256,256]{2,1,0:T(8,128)(2,1)S(1)}, u32[]{:S(2)}, u32[]{:S(2)}) %collective-permute-start.3) | collective-permute-done | bytes 262176 | tf_op jit(solution)/shard_map/ppermute | solution.py:16
  54.9 5.3 %exponential_reduce_fusion.3 = (f32[4,256]{1,0:T(4,128)S(1)}, f32[4,256,1280]{1,2,0:T(8,128)}) fusion(pred[256,1280]{0,1:T(8,128)(4,1)} %fusion.28, bf16[256,16,128]{0,2,1:T(8,128)(2,1)S(1)} %bitcast.231, bf16[2,1280,256]{2,1,0:T(8,128)(2,1)S(1)} %constant_dynamic-update-slice_fusion), kind=kOutput, calls=%fused_computation.31 | convolution fusion | flops 340788480 | bytes 6164480 | tf_op jit(solution)/shard_map/sub | solution.py:26
  60.1 5.1 %exponential_reduce_fusion.1 = (f32[4,256]{1,0:T(4,128)S(1)}, f32[4,256,1280]{1,2,0:T(8,128)}) fusion(pred[256,1280]{0,1:T(8,128)(4,1)} %fusion.28, bf16[256,16,128]{0,2,1:T(8,128)(2,1)S(1)} %bitcast.232, bf16[2,1280,256]{2,1,0:T(8,128)(2,1)S(1)} %constant_dynamic-update-slice_fusion), kind=kOutput, calls=%fused_computation.27 | convolution fusion | flops 340788480 | bytes 6164480 | tf_op jit(solution)/shard_map/sub | solution.py:26
  65.3 5.1 %exponential_reduce_fusion.2 = (f32[4,256]{1,0:T(4,128)S(1)}, f32[4,256,1280]{1,2,0:T(8,128)}) fusion(pred[256,1280]{0,1:T(8,128)(4,1)} %fusion.28, bf16[256,16,128]{0,2,1:T(8,128)(2,1)S(1)} %bitcast.233, bf16[2,1280,256]{2,1,0:T(8,128)(2,1)S(1)} %constant_dynamic-update-slice_fusion), kind=kOutput, calls=%fused_computation.29 | convolution fusion | flops 340788480 | bytes 6164480 | tf_op jit(solution)/shard_map/sub | solution.py:26
  70.4 5.1 %exponential_reduce_fusion = (f32[4,256]{1,0:T(4,128)S(1)}, f32[4,256,1280]{1,2,0:T(8,128)}) fusion(pred[256,1280]{0,1:T(8,128)(4,1)} %fusion.28, bf16[256,16,128]{0,2,1:T(8,128)(2,1)S(1)} %bitcast.234, bf16[2,1280,256]{2,1,0:T(8,128)(2,1)S(1)} %constant_dynamic-update-slice_fusion), kind=kOutput, calls=%fused_computation.25 | convolution fusion | flops 340788480 | bytes 6164480 | tf_op jit(solution)/shard_map/sub | solution.py:26
  75.5 4.0 %fusion.23 = bf16[4,256,1280]{1,2,0:T(8,128)(2,1)S(1)} fusion(f32[4,256]{1,0:T(4,128)S(1)} %get-tuple-element.22, f32[4,256,1280]{1,2,0:T(8,128)} %get-tuple-element.23), kind=kLoop, calls=%fused_computation.50 | loop fusion | flops 2621440 | bytes 7868416 | tf_op jit(solution)/shard_map/convert_element_type | solution.py:28
  85.2 1.6 fusion.25
  103.4 2.5 %fusion.9 = bf16[4,256,1280]{1,2,0:T(8,128)(2,1)S(1)} fusion(f32[4,256]{1,0:T(4,128)S(1)} %bitcast.243, f32[4,256]{1,0:T(4,128)S(1)} %get-tuple-element.16, f32[4,256,1280]{1,2,0:T(8,128)S(1)} %bitcast.224, bf16[2,1280,256]{2,1,0:T(8,128)(2,1)} %copy-done.5, bf16[256,16,128]{0,2,1:T(8,128)(2,1)} %bitcast.222), kind=kOutput, calls=%fused_computation.10 | convolution fusion | flops 340787200 | bytes 8462336 | tf_op jit(solution)/shard_map/rgd,ed->gre/dot_general | solution.py:31
  108.4 1.9 collective-permute-start.4
  110.4 3.8 %collective-permute-start.7 = (bf16[2,256,256]{1,2,0:T(8,128)(2,1)S(1)}, bf16[2,256,256]{1,2,0:T(8,128)(2,1)S(1)}, u32[]{:S(2)}, u32[]{:S(2)}) collective-permute-start(bf16[2,256,256]{1,2,0:T(8,128)(2,1)S(1)} %get-tuple-element.9), channel_id=1, source_target_pairs={{4,0},{8,4},{12,8},{16,12},{20,16},{24,20},{28,24},{32,28},{36,32}... | collective-permute-start | bytes 786440 | tf_op jit(solution)/shard_map/ppermute | solution.py:16
  114.1 1.9 collective-permute-start.6
  116.1 1.9 collective-permute-start.5
  118.0 8.5 %collective-permute-done.4 = bf16[2,256,256]{1,2,0:T(8,128)(2,1)S(1)} collective-permute-done((bf16[2,256,256]{1,2,0:T(8,128)(2,1)S(1)}, bf16[2,256,256]{1,2,0:T(8,128)(2,1)S(1)}, u32[]{:S(2)}, u32[]{:S(2)}) %collective-permute-start.4) | collective-permute-done | bytes 262176 | tf_op jit(solution)/shard_map/ppermute | solution.py:16
  126.5 7.0 %collective-permute-done.7 = bf16[2,256,256]{1,2,0:T(8,128)(2,1)S(1)} collective-permute-done((bf16[2,256,256]{1,2,0:T(8,128)(2,1)S(1)}, bf16[2,256,256]{1,2,0:T(8,128)(2,1)S(1)}, u32[]{:S(2)}, u32[]{:S(2)}) %collective-permute-start.7) | collective-permute-done | bytes 262176 | tf_op jit(solution)/shard_map/ppermute | solution.py:16
  133.6 17.3 %collective-permute-done.5 = bf16[2,256,256]{1,2,0:T(8,128)(2,1)S(1)} collective-permute-done((bf16[2,256,256]{1,2,0:T(8,128)(2,1)S(1)}, bf16[2,256,256]{1,2,0:T(8,128)(2,1)S(1)}, u32[]{:S(2)}, u32[]{:S(2)}) %collective-permute-start.5) | collective-permute-done | bytes 262176 | tf_op jit(solution)/shard_map/ppermute | solution.py:16
  152.0 3.5 %all-to-all-start.1 = ((f32[2,256,256]{2,0,1:T(2,128)}), f32[2,256,256]{2,0,1:T(2,128)S(1)}, u32[]{:S(2)}, u32[]{:S(2)}) async-start(f32[2,256,256]{2,0,1:T(2,128)} %copy.141), calls=%async_computation.1 | async-start | bytes 1048576 | tf_op jit(solution)/shard_map/all_to_all | solution.py:97
  155.5 2.4 %fusion.44 = bf16[256,4,128]{0,2,1:T(8,128)(2,1)S(1)} fusion(bf16[4,256,1280]{1,2,0:T(8,128)(2,1)} %copy-done.3, bf16[2,1280,256]{2,1,0:T(8,128)(2,1)} %copy-done.5), kind=kOutput, calls=%fused_computation.83 | convolution fusion | flops 335806464 | bytes 3211264 | tf_op jit(solution)/shard_map/gre,ed->rgd/dot_general | solution.py:35
  157.9 6.4 %all-to-all-done.1 = f32[2,256,256]{2,0,1:T(2,128)S(1)} async-done(((f32[2,256,256]{2,0,1:T(2,128)}), f32[2,256,256]{2,0,1:T(2,128)S(1)}, u32[]{:S(2)}, u32[]{:S(2)}) %all-to-all-start.1) | async-done | bytes 524320 | tf_op jit(solution)/shard_map/all_to_all | solution.py:97
  165.7 1.9 copy.144
  167.6 4.3 %all-to-all-start.2 = ((f32[2,4,16,1024]{3,2,0,1:T(8,128)}), f32[2,4,16,1024]{3,2,0,1:T(8,128)S(1)}, u32[]{:S(2)}, u32[]{:S(2)}) async-start(f32[2,4,16,1024]{3,2,0,1:T(8,128)} %copy.144), calls=%async_computation.2 | async-start | bytes 1048576 | tf_op jit(solution)/shard_map/all_to_all | solution.py:101
  171.9 3.2 %fusion.42 = bf16[256,4,128]{0,2,1:T(8,128)(2,1)} fusion(bf16[4,256,1280]{1,2,0:T(8,128)(2,1)} %copy-done.2, bf16[2,1280,256]{2,1,0:T(8,128)(2,1)} %copy-done.5), kind=kOutput, calls=%fused_computation.81 | convolution fusion | flops 335806464 | bytes 3211264 | tf_op jit(solution)/shard_map/gre,ed->rgd/dot_general | solution.py:35
  175.1 2.2 %fusion.43 = bf16[256,4,128]{0,2,1:T(8,128)(2,1)} fusion(bf16[4,256,1280]{1,2,0:T(8,128)(2,1)S(1)} %copy-done.1, bf16[2,1280,256]{2,1,0:T(8,128)(2,1)} %copy-done.5), kind=kOutput, calls=%fused_computation.82 | convolution fusion | flops 335806464 | bytes 3211264 | tf_op jit(solution)/shard_map/gre,ed->rgd/dot_general | solution.py:35
  177.4 3.7 %all-to-all-done.2 = f32[2,4,16,1024]{3,2,0,1:T(8,128)S(1)} async-done(((f32[2,4,16,1024]{3,2,0,1:T(8,128)}), f32[2,4,16,1024]{3,2,0,1:T(8,128)S(1)}, u32[]{:S(2)}, u32[]{:S(2)}) %all-to-all-start.2) | async-done | bytes 524320 | tf_op jit(solution)/shard_map/all_to_all | solution.py:101
  183.3 4.1 %collective-permute-done.8 = f32[2,16,1024]{2,1,0:T(8,128)S(1)} collective-permute-done((f32[2,16,1024]{2,1,0:T(8,128)S(1)}, f32[2,16,1024]{2,1,0:T(8,128)S(1)}, u32[]{:S(2)}, u32[]{:S(2)}) %collective-permute-start.8) | collective-permute-done | bytes 131104 | tf_op jit(solution)/shard_map/ppermute | solution.py:110
  189.0 3.2 %collective-permute-start.10 = (f32[2,16,1024]{2,1,0:T(8,128)S(1)}, f32[2,16,1024]{2,1,0:T(8,128)S(1)}, u32[]{:S(2)}, u32[]{:S(2)}) collective-permute-start(f32[2,16,1024]{2,1,0:T(8,128)S(1)} %copy-done.16), channel_id=1, source_target_pairs={{0,192},{64,0},{128,64},{192,128},{1,193},{65,1},{129,65},{193,129... | collective-permute-start | bytes 393224 | tf_op jit(solution)/shard_map/ppermute | solution.py:112
  (119 shorter events, 48.7 us)
Async XLA Ops:
  0.6 20.7 %copy-start.12 = (bf16[1,256,2048]{2,1,0:T(8,128)(2,1)S(1)}, bf16[1,256,2048]{2,1,0:T(8,128)(2,1)}, u32[]{:S(2)}) copy-start(bf16[1,256,2048]{2,1,0:T(8,128)(2,1)} %param.4) | copy-start | bytes 3145732
  3.1 9.4 %all-to-all-start = ((bf16[4,2,16384]{2,1,0:T(2,128)(2,1)}), bf16[4,2,16384]{2,1,0:T(2,128)(2,1)S(1)}, u32[]{:S(2)}, u32[]{:S(2)}) async-start(bf16[4,2,16384]{2,1,0:T(2,128)(2,1)} %reshape.113), calls=%async_computation | async-start | bytes 524288 | tf_op jit(solution)/shard_map/all_to_all | solution.py:47
  13.9 24.5 %collective-permute-start = (bf16[2,256,256]{2,1,0:T(8,128)(2,1)}, bf16[2,256,256]{2,1,0:T(8,128)(2,1)}, u32[]{:S(2)}, u32[]{:S(2)}) collective-permute-start(bf16[2,256,256]{2,1,0:T(8,128)(2,1)} %bitcast.2), channel_id=1, source_target_pairs={{0,16},{4,20},{8,24},{12,28},{16,32},{20,36},{24,40},{28,44},{32,4... | collective-permute-start | bytes 786440 | tf_op jit(solution)/shard_map/ppermute | solution.py:16
  21.9 80.5 %copy-start.4 = (bf16[1,256,2048]{1,2,0:T(8,128)(2,1)}, bf16[1,256,2048]{1,2,0:T(8,128)(2,1)S(1)}, u32[]{:S(2)}) copy-start(bf16[1,256,2048]{1,2,0:T(8,128)(2,1)S(1)} %copy.97) | copy-start | bytes 3145732
  21.9 28.7 %collective-permute-start.2 = (bf16[2,256,256]{2,1,0:T(8,128)(2,1)}, bf16[2,256,256]{2,1,0:T(8,128)(2,1)}, u32[]{:S(2)}, u32[]{:S(2)}) collective-permute-start(bf16[2,256,256]{2,1,0:T(8,128)(2,1)} %bitcast.2), channel_id=1, source_target_pairs={{0,8},{4,12},{8,16},{12,20},{16,24},{20,28},{24,32},{28,36},{32,40... | collective-permute-start | bytes 786440 | tf_op jit(solution)/shard_map/ppermute | solution.py:16
  24.8 24.8 %collective-permute-start.1 = (bf16[2,256,256]{2,1,0:T(8,128)(2,1)}, bf16[2,256,256]{2,1,0:T(8,128)(2,1)}, u32[]{:S(2)}, u32[]{:S(2)}) collective-permute-start(bf16[2,256,256]{2,1,0:T(8,128)(2,1)} %bitcast.2), channel_id=1, source_target_pairs={{0,12},{4,16},{8,20},{12,24},{16,28},{20,32},{24,36},{28,40},{32,4... | collective-permute-start | bytes 786440 | tf_op jit(solution)/shard_map/ppermute | solution.py:16
  29.6 60.7 %copy-start.6 = (bf16[1,256,2048]{1,2,0:T(8,128)(2,1)}, bf16[1,256,2048]{1,2,0:T(8,128)(2,1)S(1)}, u32[]{:S(2)}) copy-start(bf16[1,256,2048]{1,2,0:T(8,128)(2,1)S(1)} %copy.95) | copy-start | bytes 3145732
  33.1 20.8 %collective-permute-start.3 = (bf16[2,256,256]{2,1,0:T(8,128)(2,1)}, bf16[2,256,256]{2,1,0:T(8,128)(2,1)S(1)}, u32[]{:S(2)}, u32[]{:S(2)}) collective-permute-start(bf16[2,256,256]{2,1,0:T(8,128)(2,1)} %bitcast.2), channel_id=1, source_target_pairs={{0,4},{4,8},{8,12},{12,16},{16,20},{20,24},{24,28},{28,32},{32,36}... | collective-permute-start | bytes 786440 | tf_op jit(solution)/shard_map/ppermute | solution.py:16
  54.9 46.2 %copy-start.5 = (bf16[2,1280,256]{2,1,0:T(8,128)(2,1)}, bf16[2,1280,256]{2,1,0:T(8,128)(2,1)S(1)}, u32[]{:S(2)}) copy-start(bf16[2,1280,256]{2,1,0:T(8,128)(2,1)S(1)} %constant_dynamic-update-slice_fusion) | copy-start | bytes 3932164
  75.5 6.3 %slice-start.6 = ((s8[5242880]{0:T(1024)(128)(4,1)}), s8[4194304]{0:T(1024)(128)(4,1)S(1)}, s32[]{:S(2)}) async-start(s8[5242880]{0:T(1024)(128)(4,1)} %bitcast.229), calls=%async_computation.9 | async-start | bytes 8388608
  79.5 2.3 %slice-start.7 = ((s8[5242880]{0:T(1024)(128)(4,1)}), s8[1048576]{0:T(1024)(128)(4,1)S(1)}, s32[]{:S(2)}) async-start(s8[5242880]{0:T(1024)(128)(4,1)} %bitcast.229), calls=%async_computation.10 | async-start | bytes 2097152
  81.8 2.7 %slice-start.4 = ((s8[5242880]{0:T(1024)(128)(4,1)}), s8[4194304]{0:T(1024)(128)(4,1)S(1)}, s32[]{:S(2)}) async-start(s8[5242880]{0:T(1024)(128)(4,1)} %bitcast.227), calls=%async_computation.7 | async-start | bytes 8388608
  81.8 3.4 %slice-start.5 = ((s8[5242880]{0:T(1024)(128)(4,1)}), s8[1048576]{0:T(1024)(128)(4,1)S(1)}, s32[]{:S(2)}) async-start(s8[5242880]{0:T(1024)(128)(4,1)} %bitcast.227), calls=%async_computation.8 | async-start | bytes 2097152
  89.1 2.8 %slice-start.2 = ((s8[5242880]{0:T(1024)(128)(4,1)}), s8[4194304]{0:T(1024)(128)(4,1)S(1)}, s32[]{:S(2)}) async-start(s8[5242880]{0:T(1024)(128)(4,1)} %bitcast.225), calls=%async_computation.5 | async-start | bytes 8388608
  89.1 3.4 %slice-start.3 = ((s8[5242880]{0:T(1024)(128)(4,1)}), s8[1048576]{0:T(1024)(128)(4,1)S(1)}, s32[]{:S(2)}) async-start(s8[5242880]{0:T(1024)(128)(4,1)} %bitcast.225), calls=%async_computation.6 | async-start | bytes 2097152
  96.2 2.4 %slice-start = ((s8[5242880]{0:T(1024)(128)(4,1)}), s8[4194304]{0:T(1024)(128)(4,1)S(1)}, s32[]{:S(2)}) async-start(s8[5242880]{0:T(1024)(128)(4,1)} %bitcast.223), calls=%async_computation.3 | async-start | bytes 8388608
  96.3 3.4 %slice-start.1 = ((s8[5242880]{0:T(1024)(128)(4,1)}), s8[1048576]{0:T(1024)(128)(4,1)S(1)}, s32[]{:S(2)}) async-start(s8[5242880]{0:T(1024)(128)(4,1)} %bitcast.223), calls=%async_computation.4 | async-start | bytes 2097152
  97.4 8.5 %copy-start = (bf16[4,256,1280]{1,2,0:T(8,128)(2,1)}, bf16[4,256,1280]{1,2,0:T(8,128)(2,1)S(1)}, u32[]{:S(2)}) copy-start(bf16[4,256,1280]{1,2,0:T(8,128)(2,1)S(1)} %fusion.13) | copy-start | bytes 7864324
  103.4 2.6 %copy-start.7 = (bf16[1,256,2048]{1,2,0:T(8,128)(2,1)S(1)}, bf16[1,256,2048]{1,2,0:T(8,128)(2,1)}, u32[]{:S(2)}) copy-start(bf16[1,256,2048]{1,2,0:T(8,128)(2,1)} %copy-done.6) | copy-start | bytes 3145732
  108.4 18.1 %collective-permute-start.4 = (bf16[2,256,256]{1,2,0:T(8,128)(2,1)S(1)}, bf16[2,256,256]{1,2,0:T(8,128)(2,1)S(1)}, u32[]{:S(2)}, u32[]{:S(2)}) collective-permute-start(bf16[2,256,256]{1,2,0:T(8,128)(2,1)S(1)} %get-tuple-element.8), channel_id=1, source_target_pairs={{16,0},{20,4},{24,8},{28,12},{32,16},{36,20},{40,24},{44,28},{48,3... | collective-permute-start | bytes 786440 | tf_op jit(solution)/shard_map/ppermute | solution.py:16
  110.4 23.2 %collective-permute-start.7 = (bf16[2,256,256]{1,2,0:T(8,128)(2,1)S(1)}, bf16[2,256,256]{1,2,0:T(8,128)(2,1)S(1)}, u32[]{:S(2)}, u32[]{:S(2)}) collective-permute-start(bf16[2,256,256]{1,2,0:T(8,128)(2,1)S(1)} %get-tuple-element.9), channel_id=1, source_target_pairs={{4,0},{8,4},{12,8},{16,12},{20,16},{24,20},{28,24},{32,28},{36,32}... | collective-permute-start | bytes 786440 | tf_op jit(solution)/shard_map/ppermute | solution.py:16
  114.1 19.4 %collective-permute-start.6 = (bf16[2,256,256]{1,2,0:T(8,128)(2,1)S(1)}, bf16[2,256,256]{1,2,0:T(8,128)(2,1)S(1)}, u32[]{:S(2)}, u32[]{:S(2)}) collective-permute-start(bf16[2,256,256]{1,2,0:T(8,128)(2,1)S(1)} %get-tuple-element.10), channel_id=1, source_target_pairs={{8,0},{12,4},{16,8},{20,12},{24,16},{28,20},{32,24},{36,28},{40,32... | collective-permute-start | bytes 786440 | tf_op jit(solution)/shard_map/ppermute | solution.py:16
  116.1 34.8 %collective-permute-start.5 = (bf16[2,256,256]{1,2,0:T(8,128)(2,1)S(1)}, bf16[2,256,256]{1,2,0:T(8,128)(2,1)S(1)}, u32[]{:S(2)}, u32[]{:S(2)}) collective-permute-start(bf16[2,256,256]{1,2,0:T(8,128)(2,1)S(1)} %get-tuple-element.11), channel_id=1, source_target_pairs={{12,0},{16,4},{20,8},{24,12},{28,16},{32,20},{36,24},{40,28},{44,3... | collective-permute-start | bytes 786440 | tf_op jit(solution)/shard_map/ppermute | solution.py:16
  152.0 12.3 %all-to-all-start.1 = ((f32[2,256,256]{2,0,1:T(2,128)}), f32[2,256,256]{2,0,1:T(2,128)S(1)}, u32[]{:S(2)}, u32[]{:S(2)}) async-start(f32[2,256,256]{2,0,1:T(2,128)} %copy.141), calls=%async_computation.1 | async-start | bytes 1048576 | tf_op jit(solution)/shard_map/all_to_all | solution.py:97
  167.6 13.5 %all-to-all-start.2 = ((f32[2,4,16,1024]{3,2,0,1:T(8,128)}), f32[2,4,16,1024]{3,2,0,1:T(8,128)S(1)}, u32[]{:S(2)}, u32[]{:S(2)}) async-start(f32[2,4,16,1024]{3,2,0,1:T(8,128)} %copy.144), calls=%async_computation.2 | async-start | bytes 1048576 | tf_op jit(solution)/shard_map/all_to_all | solution.py:101
  171.9 3.2 %copy-start.1 = (bf16[4,256,1280]{1,2,0:T(8,128)(2,1)S(1)}, bf16[4,256,1280]{1,2,0:T(8,128)(2,1)}, u32[]{:S(2)}) copy-start(bf16[4,256,1280]{1,2,0:T(8,128)(2,1)} %copy-done) | copy-start | bytes 7864324
  181.1 6.3 %copy-start.13 = (bf16[256,4,128]{0,2,1:T(8,128)(2,1)S(1)}, bf16[256,4,128]{0,2,1:T(8,128)(2,1)}, u32[]{:S(2)}) copy-start(bf16[256,4,128]{0,2,1:T(8,128)(2,1)} %fusion.42) | copy-start | bytes 786436
  181.1 6.3 %copy-start.14 = (bf16[256,4,128]{0,2,1:T(8,128)(2,1)S(1)}, bf16[256,4,128]{0,2,1:T(8,128)(2,1)}, u32[]{:S(2)}) copy-start(bf16[256,4,128]{0,2,1:T(8,128)(2,1)} %fusion.43) | copy-start | bytes 786436
  181.1 6.3 %copy-start.15 = (f32[2,16,1024]{2,1,0:T(8,128)}, f32[2,16,1024]{2,1,0:T(8,128)S(1)}, u32[]{:S(2)}) copy-start(f32[2,16,1024]{2,1,0:T(8,128)S(1)} %fusion.78) | copy-start | bytes 393220
  181.1 6.3 %collective-permute-start.8 = (f32[2,16,1024]{2,1,0:T(8,128)S(1)}, f32[2,16,1024]{2,1,0:T(8,128)S(1)}, u32[]{:S(2)}, u32[]{:S(2)}) collective-permute-start(f32[2,16,1024]{2,1,0:T(8,128)S(1)} %fusion.78), channel_id=1, source_target_pairs={{0,64},{64,128},{128,192},{192,0},{1,65},{65,129},{129,193},{193,1... | collective-permute-start | bytes 393224 | tf_op jit(solution)/shard_map/ppermute | solution.py:110
  187.4 6.2 %collective-permute-start.9 = (f32[2,16,1024]{2,1,0:T(8,128)S(1)}, f32[2,16,1024]{2,1,0:T(8,128)S(1)}, u32[]{:S(2)}, u32[]{:S(2)}) collective-permute-start(f32[2,16,1024]{2,1,0:T(8,128)S(1)} %collective-permute-done.8), channel_id=1, source_target_pairs={{0,64},{64,128},{128,192},{192,0},{1,65},{65,129},{129,193},{193,1... | collective-permute-start | bytes 393224 | tf_op jit(solution)/shard_map/ppermute | solution.py:110
  189.0 5.7 %collective-permute-start.10 = (f32[2,16,1024]{2,1,0:T(8,128)S(1)}, f32[2,16,1024]{2,1,0:T(8,128)S(1)}, u32[]{:S(2)}, u32[]{:S(2)}) collective-permute-start(f32[2,16,1024]{2,1,0:T(8,128)S(1)} %copy-done.16), channel_id=1, source_target_pairs={{0,192},{64,0},{128,64},{192,128},{1,193},{65,1},{129,65},{193,129... | collective-permute-start | bytes 393224 | tf_op jit(solution)/shard_map/ppermute | solution.py:112
  (7 other events, 9.5 us)
